TPU v7x, 256 devices: a whole 4x4x8 slice. The times are simulated.
256 devices in a mesh: req: 32 (over x, z), mlp: 8 (over y, core).
Axes of the slice: x: 4, y: 4, z: 8, core: 2. Of those that a mesh axis runs over, the one named last changes fastest.
Arguments:
- x_pages: bfloat16 [1024, 8, 4096], P('req', None, 'mlp'), may hold values from -6 to 6
- page_owner: int32 [1024], P('req'), may hold values from 0 to 31, as said below
- request_id: int32 [8192], P('req'), may hold values from 0 to 8191, as said below
- adapter_table: int32 [8192], P('req'), may hold values from 0 to 63
- ln_gain: float32 [4096], replicated, may hold values from 0.5 to 1.5
- ln_bias: float32 [4096], replicated, may hold values from -3 to 3
- w_query: bfloat16 [4096, 2048], P('req', 'mlp'), may hold values from -0.09375 to 0.09375
- w_key: bfloat16 [4096, 2048], P('req', 'mlp'), may hold values from -0.09375 to 0.09375
- w_value: bfloat16 [4096, 2048], P('req', 'mlp'), may hold values from -0.09375 to 0.09375
- w_attn_out: bfloat16 [2048, 4096], P('mlp', 'req'), may hold values from -0.125 to 0.125
- down_query: bfloat16 [4096, 1024], P('mlp'), may hold values from -0.09375 to 0.09375
- up_query: bfloat16 [1024, 2048], P(None, 'mlp'), may hold values from -1.5 to 1.5
- down_value: bfloat16 [4096, 1024], P('mlp'), may hold values from -0.09375 to 0.09375
- up_value: bfloat16 [1024, 2048], P(None, 'mlp'), may hold values from -1.5 to 1.5
- w_fc_in: bfloat16 [4096, 8192], P('req', 'mlp'), may hold values from -0.09375 to 0.09375
- b_fc_in: float32 [8192], P('mlp'), may hold values from -3 to 3
- down_fc: bfloat16 [4096, 1024], P('mlp'), may hold values from -0.09375 to 0.09375
- up_fc: bfloat16 [1024, 8192], P(None, 'mlp'), may hold values from -1.5 to 1.5
- w_fc_out: bfloat16 [8192, 4096], P('mlp', 'req'), may hold values from -0.0625 to 0.0625
- b_fc_out: float32 [4096], P('mlp'), may hold values from -3 to 3
Outputs:
- out_pages: bfloat16 [1024, 8, 4096], P('req', None, 'mlp')
Inputs may be any that keep to these rules, and one draw needn't show every extreme that they name: `page_owner`: every owner receives exactly 32 pages, at most 2 of them from one device, and some device sends exactly 2 pages to some owner. `request_id`: ids never fall; every request lies inside one owner's block of 256 rows, and the ids of block k lie in k * 256 to k * 256 + 255; some request is 256 long.
All inputs are finite; a program needn't handle non-finite values.
Results may differ from a plain program's by a relative error of at most 0.006.
Values may be sent and summed in bfloat16 or wider, within the bound.
No kernel may reach another device: no remote copies, remote signals or barrier semaphores. Data moves between devices by JAX's collectives and lax.ppermute only.
A program may use at most 128 MiB of HBM per device.

v0:
```python
import jax
import jax.numpy as jnp
from jax import lax
from jax.sharding import PartitionSpec as P

HS = 256
ROT = 64
NAD = 64
R = 16
EPS = 1e-05


def gelu_tanh(v):
    return 0.5 * v * (1.0 + jnp.tanh(0.7978845608028654 * (v + 0.044715 * v * v * v)))


def rotate(block, pos):
    half = ROT // 2
    freq = jnp.power(10000.0, -jnp.arange(half).astype(jnp.float32) * 2.0 / ROT)
    angle = pos.astype(jnp.float32)[:, None, None] * freq[None, None, :]
    cosine = jnp.cos(angle)
    sine = jnp.sin(angle)
    even = block[:, :, 0:ROT:2]
    odd = block[:, :, 1:ROT:2]
    turned = jnp.stack([even * cosine - odd * sine, odd * cosine + even * sine], axis=-1)
    turned = turned.reshape(block.shape[0], block.shape[1], ROT)
    return jnp.concatenate([turned, block[:, :, ROT:]], axis=2)


def on_device(
    x_pages,
    page_owner,
    request_id,
    adapter_table,
    ln_gain,
    ln_bias,
    w_query,
    w_key,
    w_value,
    w_attn_out,
    down_query,
    up_query,
    down_value,
    up_value,
    w_fc_in,
    b_fc_in,
    down_fc,
    up_fc,
    w_fc_out,
    b_fc_out,
):
    groups = lax.axis_size("req")
    pg_dev = x_pages.shape[0]
    page_len = x_pages.shape[1]
    width_m = x_pages.shape[2]
    tok = request_id.shape[0]
    per_owner = pg_dev // groups + 1
    slots = groups * per_owner
    page_iota = jnp.arange(pg_dev)
    earlier = (page_owner[None, :] == page_owner[:, None]) & (
        page_iota[None, :] < page_iota[:, None]
    )
    rank = jnp.sum(earlier.astype(jnp.int32), axis=1)
    slot = page_owner * per_owner + rank
    place = (slot[None, :] == jnp.arange(slots)[:, None]).astype(jnp.bfloat16)
    flat_pages = x_pages.reshape(pg_dev, page_len * width_m)
    outgoing = jnp.dot(place, flat_pages, preferred_element_type=jnp.float32).astype(jnp.bfloat16)
    outgoing = outgoing.reshape(groups, per_owner, page_len * width_m)
    filled = jnp.sum(place, axis=1).reshape(groups, per_owner)
    arrived, marks = (
        lax.all_to_all(outgoing, "req", split_axis=0, concat_axis=0, tiled=True),
        lax.all_to_all(filled, "req", split_axis=0, concat_axis=0, tiled=True),
    )
    valid = marks.reshape(slots).astype(jnp.float32)
    position = jnp.cumsum(valid) - 1.0
    take = (
        (position[None, :] == jnp.arange(pg_dev).astype(jnp.float32)[:, None])
        & (valid[None, :] > 0.5)
    ).astype(jnp.bfloat16)
    own_x = jnp.dot(
        take, arrived.reshape(slots, page_len * width_m), preferred_element_type=jnp.float32
    )
    own_x = own_x.astype(jnp.bfloat16).reshape(tok, width_m)
    column = lax.axis_index("mlp") * width_m
    n_mlp = lax.axis_size("mlp")
    copies = jnp.broadcast_to(own_x[None], (n_mlp, tok, width_m))
    spread_x = lax.all_to_all(copies, "mlp", split_axis=0, concat_axis=0, tiled=True)
    whole = jnp.transpose(spread_x, (1, 0, 2)).reshape(tok, n_mlp * width_m).astype(jnp.float32)
    mean = jnp.mean(whole, axis=1, keepdims=True)
    var = jnp.mean(jnp.square(whole - mean), axis=1, keepdims=True)
    full_ln = ((whole - mean) * lax.rsqrt(var + EPS) * ln_gain + ln_bias).astype(jnp.bfloat16)
    ln_m = lax.dynamic_slice_in_dim(full_ln, column, width_m, 1)
    local_req = request_id - lax.axis_index("req") * tok
    lookup = local_req[:, None] == jnp.arange(tok)[None, :]
    adapter = jnp.sum(jnp.where(lookup, adapter_table[None, :], 0), axis=1)
    onehot = (adapter[:, None] == jnp.arange(NAD)[None, :]).astype(jnp.float32)
    onehot_low = onehot.astype(jnp.bfloat16)

    def pick(down):
        spread = jnp.dot(ln_m, down, preferred_element_type=jnp.float32).reshape(tok, NAD, R)
        return jnp.sum(spread * onehot[:, :, None], axis=1)

    picked = lax.psum((pick(down_query), pick(down_value), pick(down_fc)), "mlp")

    def lift(chosen, up):
        expanded = (onehot_low[:, :, None] * chosen.astype(jnp.bfloat16)[:, None, :]).reshape(
            tok, NAD * R
        )
        return jnp.dot(expanded, up, preferred_element_type=jnp.float32)

    row_iota = jnp.arange(tok)
    start = jnp.sum((request_id[None, :] < request_id[:, None]).astype(jnp.int32), axis=1)
    pos = row_iota - start
    mask = (request_id[:, None] == request_id[None, :]) & (row_iota[None, :] <= row_iota[:, None])
    heads_w = w_query.shape[1]
    ff_w = w_fc_in.shape[1]
    packed = jnp.concatenate([w_query, w_key, w_value, w_fc_in, w_attn_out.T], axis=1)
    fo_copies = jnp.broadcast_to(w_fc_out[None], (groups,) + w_fc_out.shape)
    fo_rows = lax.all_to_all(fo_copies, "req", split_axis=0, concat_axis=0, tiled=True)
    gathered = lax.all_gather(packed, "req", axis=0, tiled=True)
    n_in = 3 * heads_w + ff_w
    base = jnp.dot(full_ln, gathered[:, :n_in], preferred_element_type=jnp.float32)
    base_q = base[:, :heads_w]
    base_k = base[:, heads_w : 2 * heads_w]
    base_v = base[:, 2 * heads_w : 3 * heads_w]
    query = rotate(
        (base_q + lift(picked[0], up_query)).reshape(tok, heads_w // HS, HS), pos
    ).astype(jnp.bfloat16)
    keys = rotate(base_k.reshape(tok, heads_w // HS, HS), pos).astype(jnp.bfloat16)
    value = (
        (base_v + lift(picked[1], up_value)).astype(jnp.bfloat16).reshape(tok, heads_w // HS, HS)
    )
    scores = jnp.einsum("qhd,khd->hqk", query, keys, preferred_element_type=jnp.float32) * HS ** (
        -0.5
    )
    scores = jnp.where(mask[None, :, :], scores, -1e30)
    top = jnp.max(scores, axis=2, keepdims=True)
    weights = jnp.exp(scores - top)
    probs = (weights / jnp.sum(weights, axis=2, keepdims=True)).astype(jnp.bfloat16)
    mixed_heads = jnp.einsum("hqk,khd->qhd", probs, value, preferred_element_type=jnp.float32)
    attn = mixed_heads.astype(jnp.bfloat16).reshape(tok, heads_w)
    hidden_pre = base[:, 3 * heads_w :]
    hidden_pre = hidden_pre + lift(picked[2], up_fc) + b_fc_in
    hidden = gelu_tanh(hidden_pre).astype(jnp.bfloat16)
    part = lax.dot_general(
        attn, gathered[:, n_in:], (((1,), (1,)), ((), ())), preferred_element_type=jnp.float32
    )
    part = part + jnp.einsum(
        "tf,rfc->trc", hidden, fo_rows, preferred_element_type=jnp.float32
    ).reshape(tok, groups * fo_rows.shape[2])
    shares = lax.psum_scatter(part, "mlp", scatter_dimension=1, tiled=True)
    result = (own_x.astype(jnp.float32) + shares + b_fc_out).astype(jnp.bfloat16)
    back_flat = result.reshape(pg_dev, page_len * width_m)
    leaving = jnp.dot(take.T, back_flat, preferred_element_type=jnp.float32).astype(jnp.bfloat16)
    leaving = leaving.reshape(groups, per_owner, page_len * width_m)
    returned = lax.all_to_all(leaving, "req", split_axis=0, concat_axis=0, tiled=True)
    pages_back = jnp.dot(
        place.T, returned.reshape(slots, page_len * width_m), preferred_element_type=jnp.float32
    )
    return pages_back.astype(jnp.bfloat16).reshape(pg_dev, page_len, width_m)


def solution(mesh):
    in_specs = (
        P("req", None, "mlp"),
        P("req"),
        P("req"),
        P("req"),
        P(),
        P(),
        P("req", "mlp"),
        P("req", "mlp"),
        P("req", "mlp"),
        P("mlp", "req"),
        P("mlp", None),
        P(None, "mlp"),
        P("mlp", None),
        P(None, "mlp"),
        P("req", "mlp"),
        P("mlp"),
        P("mlp", None),
        P(None, "mlp"),
        P("mlp", "req"),
        P("mlp"),
    )
    out_specs = P("req", None, "mlp")
    return jax.shard_map(
        on_device, mesh=mesh, in_specs=in_specs, out_specs=out_specs, check_vma=False
    )
```

profile of v0, /device:TPU:57, one launch (start us, length us, event | category | flops | bytes accessed | tf_op | source)
XLA Modules:
  0.0 442.5 jit_solution(15995266762931642183)
XLA Ops:
  6.5 1.0 constant_dynamic-update-slice_fusion.3
  7.5 0.9 copy.61
  8.5 0.8 constant_dynamic-update-slice_fusion.2
  9.3 0.8 constant_dynamic-update-slice_fusion.1
  10.2 1.0 constant_dynamic-update-slice_fusion
  11.2 0.8 copy-done.6
  12.0 0.9 convert_reduce_fusion.3
  12.9 0.7 multiply_add_fusion.1
  13.7 0.7 all_to_all.24
  14.4 10.6 %all-to-all-start = ((bf16[32,1,2]{2,1,0:T(2,128)(2,1)}), bf16[32,1,2]{2,1,0:T(2,128)(2,1)S(1)}, u32[]{:S(2)}, u32[]{:S(2)}) async-start(bf16[32,1,2]{2,1,0:T(2,128)(2,1)} %all_to_all.24), calls=%async_computation | async-start | bytes 32768 | tf_op jit(solution)/shard_map/all_to_all | solution.py:72
  25.0 1.0 copy.77
  26.1 0.4 convolution_convert_fusion.1
  26.5 1.1 reshape.352
  27.6 5.2 %all-to-all-done = bf16[32,1,2]{2,1,0:T(2,128)(2,1)S(1)} async-done(((bf16[32,1,2]{2,1,0:T(2,128)(2,1)}), bf16[32,1,2]{2,1,0:T(2,128)(2,1)S(1)}, u32[]{:S(2)}, u32[]{:S(2)}) %all-to-all-start) | async-done | bytes 160 | tf_op jit(solution)/shard_map/all_to_all | solution.py:72
  32.8 4.6 %all-to-all-start.1 = ((bf16[32,2,4096]{2,1,0:T(2,128)(2,1)}), bf16[32,2,4096]{2,1,0:T(2,128)(2,1)S(1)}, u32[]{:S(2)}, u32[]{:S(2)}) async-start(bf16[32,2,4096]{2,1,0:T(2,128)(2,1)} %reshape.352), calls=%async_computation.1 | async-start | bytes 1048576 | tf_op jit(solution)/shard_map/all_to_all | solution.py:71
  38.0 21.4 %all-to-all-done.1 = bf16[32,2,4096]{2,1,0:T(2,128)(2,1)S(1)} async-done(((bf16[32,2,4096]{2,1,0:T(2,128)(2,1)}), bf16[32,2,4096]{2,1,0:T(2,128)(2,1)S(1)}, u32[]{:S(2)}, u32[]{:S(2)}) %all-to-all-start.1) | async-done | bytes 524320 | tf_op jit(solution)/shard_map/all_to_all | solution.py:71
  59.4 0.2 reshape.353
  59.6 0.3 convolution_convert_fusion.3
  59.9 0.1 reshape.354
  60.0 0.1 copy.60
  60.2 1.5 broadcast_in_dim.15
  61.7 7.6 %all-to-all-start.2 = ((bf16[8,256,512]{1,2,0:T(8,128)(2,1)}), bf16[8,256,512]{1,2,0:T(8,128)(2,1)}, u32[]{:S(2)}, u32[]{:S(2)}) async-start(bf16[8,256,512]{1,2,0:T(8,128)(2,1)} %broadcast_in_dim.15), calls=%async_computation.2 | async-start | bytes 4194304 | tf_op jit(solution)/shard_map/all_to_all | solution.py:87
  69.3 0.1 copy.70
  69.4 24.5 %all-to-all-done.2 = bf16[8,256,512]{1,2,0:T(8,128)(2,1)} async-done(((bf16[8,256,512]{1,2,0:T(8,128)(2,1)}), bf16[8,256,512]{1,2,0:T(8,128)(2,1)}, u32[]{:S(2)}, u32[]{:S(2)}) %all-to-all-start.2) | async-done | bytes 2097184 | tf_op jit(solution)/shard_map/all_to_all | solution.py:87
  93.9 4.3 broadcast_in_dim.19
  98.2 4.9 %all-to-all-start.3 = ((bf16[32,1024,128]{1,2,0:T(8,128)(2,1)}), bf16[32,1024,128]{1,2,0:T(8,128)(2,1)}, u32[]{:S(2)}, u32[]{:S(2)}) async-start(bf16[32,1024,128]{1,2,0:T(8,128)(2,1)} %broadcast_in_dim.19), calls=%async_computation.3 | async-start | bytes 16777216 | tf_op jit(solution)/shard_map/all_to_all | solution.py:119
  103.1 0.5 multiply_power_fusion
  103.7 0.1 convert_reduce_fusion.1
  103.8 0.2 select_reduce_fusion
  104.0 0.6 subtract_convert_fusion
  104.6 2.3 convert_reduce_fusion
  106.9 2.3 multiply_reduce_fusion
  109.2 2.6 fusion.5
  111.8 0.6 fusion.27
  112.4 0.6 fusion.25
  113.0 0.6 fusion.29
  113.5 0.4 multiply_reduce_fusion.2
  114.0 25.8 %all-reduce = (bf16[256,16]{0,1:T(8,128)(2,1)S(1)}, bf16[256,16]{0,1:T(8,128)(2,1)S(1)}, bf16[256,16]{0,1:T(8,128)(2,1)S(1)}) all-reduce(f32[256,16]{0,1:T(8,128)S(1)} %get-tuple-element.6, f32[256,16]{0,1:T(8,128)S(1)} %get-tuple-element.7, f32[256,16]{0,1:T(8,128)S(1)} %get-tuple-element.5), channel_id=1, replica_groups=mesh['req'=32,'mlp'=8] {'mlp'}, use_global_device_ids=true, to_apply=%region_14.15 | all-reduce | flops 12288 | bytes 73728 | tf_op jit(solution)/shard_map/psum | solution.py:103
  139.8 0.9 broadcast_multiply_fusion.1
  140.7 166.7 %all-gather.2.cloned.1.call-done = bf16[4096,2048]{1,0:T(8,128)(2,1)} async-done(((bf16[128,2048]{1,0:T(8,128)(2,1)}), bf16[4096,2048]{1,0:T(8,128)(2,1)}) %all-gather.2.cloned.1.call-update) | async-done | bytes 16777232 | tf_op jit(solution)/shard_map/all_gather | solution.py:120
  307.3 8.6 %fusion = f32[256,1792]{1,0:T(8,128)S(1)} fusion(bf16[256,4096]{0,1:T(8,128)(2,1)} %copy-done.1, bf16[4096,2048]{1,0:T(8,128)(2,1)} %all-gather.2.cloned.1.call-done), kind=kOutput, calls=%fused_computation | convolution fusion | flops 3758096384 | bytes 18612224 | tf_op jit(solution)/shard_map/dot_general | solution.py:122
  315.9 1.2 copy-done.2
  317.1 0.7 slice_bitcast_fusion
  317.8 2.1 slice.46
  319.9 2.6 slice.45
  322.6 2.2 fusion.9
  324.7 2.1 slice.41
  326.8 2.1 slice.42
  328.9 1.5 fusion.60
  331.0 1.2 fusion.47
  332.2 0.3 fusion.84
  332.6 1.6 fusion.10
  334.2 12.2 %all-to-all-done.3 = bf16[32,1024,128]{1,2,0:T(8,128)(2,1)} async-done(((bf16[32,1024,128]{1,2,0:T(8,128)(2,1)}), bf16[32,1024,128]{1,2,0:T(8,128)(2,1)}, u32[]{:S(2)}, u32[]{:S(2)}) %all-to-all-start.3) | async-done | bytes 8388640 | tf_op jit(solution)/shard_map/all_to_all | solution.py:119
  346.4 8.9 %fusion.17 = f32[256,4096]{1,0:T(8,128)} fusion(bf16[1024,4096]{0,1:T(8,128)(2,1)} %bitcast.21, bf16[256,1024]{0,1:T(8,128)(2,1)S(1)} %bitcast.77, bf16[1024,1024]{1,0:T(8,128)(2,1)S(1)} %copy-done, f32[256,1792]{1,0:T(8,128)} %copy-done.2, f32[1024]{0:T(1024)S(1)} %copy-done.10), kind=kOutput, calls=%fused_computation.34 | convolution fusion | flops 2687238144 | bytes 16257024 | tf_op jit(solution)/shard_map/reshape | solution.py:150
  355.3 5.8 %convolution_add_fusion = f32[256,4096]{1,0:T(8,128)} fusion(f32[256,4096]{1,0:T(8,128)} %fusion.17, bf16[4096,2048]{1,0:T(8,128)(2,1)} %all-gather.2.cloned.1.call-done, bf16[256,256]{1,0:T(8,128)(2,1)S(1)} %fusion.10, f32[256,256]{0,1:T(8,128)S(1)} %get-tuple-element.23, f32[256]{0:T(256)S(1)} %fusion.24, f32[256]{0:T(256)S(1)} %get-tuple-element.22), kind=kOutput, calls=%fused_computation.2 | convolution fusion | flops 571736064 | bytes 10881024 | tf_op jit(solution)/shard_map/dot_general | solution.py:145
  361.1 43.3 %reduce-scatter.2.cloned.1.call-done = f32[256,512]{1,0:T(8,128)} async-done(((f32[256,4096]{1,0:T(8,128)}), f32[256,512]{1,0:T(8,128)}) %reduce-scatter.2.cloned.1.call-update) | async-done | bytes 524304 | tf_op jit(solution)/shard_map/reduce_scatter | solution.py:151
  404.4 1.1 add_convert_fusion
  405.5 0.1 reshape.362
  405.6 0.4 convolution_convert_fusion
  406.0 0.3 reshape.363
  406.4 26.9 %all_to_all.30 = bf16[32,2,4096]{2,1,0:T(2,128)(2,1)} all-to-all(bf16[32,2,4096]{2,1,0:T(2,128)(2,1)S(1)} %reshape.363), channel_id=1, replica_groups=mesh['req'=32,'mlp'=8] {'req'}, dimensions={0} | all-to-all | bytes 1048576 | tf_op jit(solution)/shard_map/all_to_all | solution.py:156
  433.3 1.2 reshape.364
  434.5 0.3 convolution_convert_fusion.2
  434.8 0.8 copy.78
  (59 shorter events, 1.4 us)
Async XLA Ops:
  6.5 339.8 %copy-start = (bf16[1024,1024]{1,0:T(8,128)(2,1)S(1)}, bf16[1024,1024]{1,0:T(8,128)(2,1)}, u32[]{:S(2)}) copy-start(bf16[1024,1024]{1,0:T(8,128)(2,1)} %param.37) | copy-start | bytes 6291460
  6.5 300.8 %all-gather.2.cloned.1.call-start = ((), (), s32[]{:S(2)}) async-start(), calls=%async_computation.6 | async-start | bytes 17301504 | tf_op jit(solution)/shard_map/all_gather | solution.py:120
  11.2 0.8 copy-start.6
  13.6 23.9 %copy-start.13 = (s32[32]{0:T(128)}, s32[32]{0:T(128)S(1)}, u32[]{:S(2)}) copy-start(s32[32]{0:T(128)S(1)} %multiply_add_fusion.1) | copy-start | bytes 388
  14.4 18.4 %all-to-all-start = ((bf16[32,1,2]{2,1,0:T(2,128)(2,1)}), bf16[32,1,2]{2,1,0:T(2,128)(2,1)S(1)}, u32[]{:S(2)}, u32[]{:S(2)}) async-start(bf16[32,1,2]{2,1,0:T(2,128)(2,1)} %all_to_all.24), calls=%async_computation | async-start | bytes 32768 | tf_op jit(solution)/shard_map/all_to_all | solution.py:72
  32.8 26.6 %all-to-all-start.1 = ((bf16[32,2,4096]{2,1,0:T(2,128)(2,1)}), bf16[32,2,4096]{2,1,0:T(2,128)(2,1)S(1)}, u32[]{:S(2)}, u32[]{:S(2)}) async-start(bf16[32,2,4096]{2,1,0:T(2,128)(2,1)} %reshape.352), calls=%async_computation.1 | async-start | bytes 1048576 | tf_op jit(solution)/shard_map/all_to_all | solution.py:71
  37.4 24.2 %copy-start.15 = (f32[32]{0:T(128)}, f32[32]{0:T(128)S(1)}, u32[]{:S(2)}) copy-start(f32[32]{0:T(128)S(1)} %iota_convert_fusion) | copy-start | bytes 388
  59.6 9.6 %copy-start.7 = (bf16[1024,128]{1,0:T(8,128)(2,1)S(1)}, bf16[1024,128]{1,0:T(8,128)(2,1)}, u32[]{:S(2)}) copy-start(bf16[1024,128]{1,0:T(8,128)(2,1)} %param.38) | copy-start | bytes 786436
  61.7 32.2 %all-to-all-start.2 = ((bf16[8,256,512]{1,2,0:T(8,128)(2,1)}), bf16[8,256,512]{1,2,0:T(8,128)(2,1)}, u32[]{:S(2)}, u32[]{:S(2)}) async-start(bf16[8,256,512]{1,2,0:T(8,128)(2,1)} %broadcast_in_dim.15), calls=%async_computation.2 | async-start | bytes 4194304 | tf_op jit(solution)/shard_map/all_to_all | solution.py:87
  98.2 5.5 %copy-start.11 = (s32[256]{0:T(256)S(1)}, s32[256]{0:T(256)}, u32[]{:S(2)}) copy-start(s32[256]{0:T(256)} %param.22) | copy-start | bytes 3076
  98.2 5.6 %copy-start.17 = (s32[256]{0:T(256)S(1)}, s32[256]{0:T(256)}, u32[]{:S(2)}) copy-start(s32[256]{0:T(256)} %param.23) | copy-start | bytes 3076
  98.2 248.2 %all-to-all-start.3 = ((bf16[32,1024,128]{1,2,0:T(8,128)(2,1)}), bf16[32,1024,128]{1,2,0:T(8,128)(2,1)}, u32[]{:S(2)}, u32[]{:S(2)}) async-start(bf16[32,1024,128]{1,2,0:T(8,128)(2,1)} %broadcast_in_dim.19), calls=%async_computation.3 | async-start | bytes 16777216 | tf_op jit(solution)/shard_map/all_to_all | solution.py:119
  103.1 6.1 %copy-start.8 = (f32[4096]{0:T(1024)S(1)}, f32[4096]{0:T(1024)}, u32[]{:S(2)}) copy-start(f32[4096]{0:T(1024)} %param.25) | copy-start | bytes 49156
  103.1 6.1 %copy-start.9 = (f32[4096]{0:T(1024)S(1)}, f32[4096]{0:T(1024)}, u32[]{:S(2)}) copy-start(f32[4096]{0:T(1024)} %param.24) | copy-start | bytes 49156
  103.1 301.3 %reduce-scatter.2.cloned.1.call-start = ((), (), s32[]{:S(2)}) async-start(), calls=%async_computation.7 | async-start | bytes 4718592 | tf_op jit(solution)/shard_map/reduce_scatter | solution.py:151
  104.6 7.2 %copy-start.3 = (bf16[512,1024]{1,0:T(8,128)(2,1)S(1)}, bf16[512,1024]{1,0:T(8,128)(2,1)}, u32[]{:S(2)}) copy-start(bf16[512,1024]{1,0:T(8,128)(2,1)} %param.30) | copy-start | bytes 3145732
  106.9 5.5 %copy-start.4 = (bf16[512,1024]{1,0:T(8,128)(2,1)S(1)}, bf16[512,1024]{1,0:T(8,128)(2,1)}, u32[]{:S(2)}) copy-start(bf16[512,1024]{1,0:T(8,128)(2,1)} %param.36) | copy-start | bytes 3145732
  109.2 3.8 copy-start.5
  111.8 2.2 copy-start.1
  315.9 1.2 copy-start.2
  317.1 29.3 %copy-start.10 = (f32[1024]{0:T(1024)S(1)}, f32[1024]{0:T(1024)}, u32[]{:S(2)}) copy-start(f32[1024]{0:T(1024)} %param.35) | copy-start | bytes 12292
  361.1 43.3 %copy-start.12 = (f32[512]{0:T(512)S(1)}, f32[512]{0:T(512)}, u32[]{:S(2)}) copy-start(f32[512]{0:T(512)} %param.39) | copy-start | bytes 6148
  361.1 44.6 %copy-start.16 = (f32[32]{0:T(128)S(1)}, f32[32]{0:T(128)}, u32[]{:S(2)}) copy-start(f32[32]{0:T(128)} %copy-done.15) | copy-start | bytes 388
  361.1 73.5 %copy-start.14 = (s32[32]{0:T(128)S(1)}, s32[32]{0:T(128)}, u32[]{:S(2)}) copy-start(s32[32]{0:T(128)} %copy-done.13) | copy-start | bytes 388
Sparse Core Ops, SparseCore 0:
  12.1 295.1 all-gather.1
  361.2 43.1 reduce-scatter.1
where the time goes:
time: 443 us; the launch traced here: 442 us
  waiting for transfers between devices  273 us (62%)
  blocking collectives  52.7 us (12%)
  matrix products  30.4 us (7%)
  local copies, waits for them, and re-layouts  29.9 us (7%)
  starting transfers between devices  27.7 us (6%)
  other arithmetic  14.7 us (3%)
  between operations  13.9 us (3%)
    all_gather x1, waiting for transfers between devices, on_device(): gathered = lax.all_gather(packed, 'req', axis=0, tiled=True)  167 us
    reduce_scatter x1, waiting for transfers between devices, on_device(): shares = lax.psum_scatter(part, 'mlp', scatter_dimension=1, tiled=True)  43.3 us
    all_to_all x1, blocking collectives, on_device(): lax.all_to_all(leaving, 'req', split_axis=0, concat_axis=0, tiled=True)  26.9 us
    psum x1, blocking collectives, on_device(): lax.psum((pick(down_query), pick(down_value), pick(down_fc)), 'mlp')  25.8 us
    all_to_all x1, waiting for transfers between devices, on_device(): lax.all_to_all(copies, 'mlp', split_axis=0, concat_axis=0, tiled=True)  24.5 us
    all_to_all x1, waiting for transfers between devices, on_device(): lax.all_to_all(outgoing, 'req', split_axis=0, concat_axis=0, tiled=True)  21.4 us
    all_to_all x1, waiting for transfers between devices, on_device(): lax.all_to_all(fo_copies, 'req', split_axis=0, concat_axis=0, tiled=True)  12.2 us
    all_to_all x1, starting transfers between devices, on_device(): lax.all_to_all(filled, 'req', split_axis=0, concat_axis=0, tiled=True)  10.6 us
  transfers between devices with their start and end apart: 6, of which 6 were waited for; matrix products, arithmetic and copies ran while one was open for 11% of the time, Pallas kernels for 0%

commit v1 on v0

--- a/solution.py
+++ b/solution.py
@@ -117,7 +117,9 @@
     packed = jnp.concatenate([w_query, w_key, w_value, w_fc_in, w_attn_out.T], axis=1)
     fo_copies = jnp.broadcast_to(w_fc_out[None], (groups,) + w_fc_out.shape)
     fo_rows = lax.all_to_all(fo_copies, "req", split_axis=0, concat_axis=0, tiled=True)
-    gathered = lax.all_gather(packed, "req", axis=0, tiled=True)
+    gathered = jnp.concatenate(
+        lax.all_to_all(jnp.stack([packed] * lax.axis_size("req")), "req", 0, 0), axis=0
+    )
     n_in = 3 * heads_w + ff_w
     base = jnp.dot(full_ln, gathered[:, :n_in], preferred_element_type=jnp.float32)
     base_q = base[:, :heads_w]

time: 443 us -> 806 us (1.82)
  waiting for transfers between devices: 273 us -> 605 us
  starting transfers between devices: 27.7 us -> 45.7 us
  blocking collectives: 52.7 us -> 62 us
    all_to_all x0 -> x1, waiting for transfers between devices: none -> 386 us  [on_device(): lax.all_to_all(jnp.stack([packed] * lax.axis_size('req')), 'req', 0, 0)]
    all_gather x1 -> x0, waiting for transfers between devices: 167 us -> none  [on_device(): gathered = lax.all_gather(packed, 'req', axis=0, tiled=True)]
    all_to_all x1, waiting for transfers between devices: 12.2 us -> 114 us  [on_device(): lax.all_to_all(fo_copies, 'req', split_axis=0, concat_axis=0, tiled=True)]
    reduce_scatter x1, waiting for transfers between devices: 43.3 us -> 59.7 us  [on_device(): shares = lax.psum_scatter(part, 'mlp', scatter_dimension=1, tiled=True)]
    all_to_all x1, starting transfers between devices: 4.88 us -> 17.6 us  [on_device(): lax.all_to_all(fo_copies, 'req', split_axis=0, concat_axis=0, tiled=True)]
    psum x1, blocking collectives: 25.8 us -> 35 us  [on_device(): lax.psum((pick(down_query), pick(down_value), pick(down_fc)), 'mlp')]
  transfers between devices with their start and end apart: 6 -> 6, of which waited for: 6 -> 6; matrix products, arithmetic and copies ran while one was open for 11% -> 5% of each run, Pallas kernels for 0% -> 0%
where the time goes in v1:
time: 806 us; the launch traced here: 805 us
  waiting for transfers between devices  605 us (75%)
  blocking collectives  62 us (8%)
  starting transfers between devices  45.7 us (6%)
  local copies, waits for them, and re-layouts  33.3 us (4%)
  matrix products  29.5 us (4%)
  other arithmetic  15.5 us (2%)
  between operations  13.9 us (2%)
    all_to_all x1, waiting for transfers between devices, on_device(): lax.all_to_all(jnp.stack([packed] * lax.axis_size('req')), 'req', 0, 0)  386 us
    all_to_all x1, waiting for transfers between devices, on_device(): lax.all_to_all(fo_copies, 'req', split_axis=0, concat_axis=0, tiled=True)  114 us
    reduce_scatter x1, waiting for transfers between devices, on_device(): shares = lax.psum_scatter(part, 'mlp', scatter_dimension=1, tiled=True)  59.7 us
    psum x1, blocking collectives, on_device(): lax.psum((pick(down_query), pick(down_value), pick(down_fc)), 'mlp')  35 us
    all_to_all x1, blocking collectives, on_device(): lax.all_to_all(leaving, 'req', split_axis=0, concat_axis=0, tiled=True)  26.9 us
    all_to_all x1, waiting for transfers between devices, on_device(): lax.all_to_all(copies, 'mlp', split_axis=0, concat_axis=0, tiled=True)  24.4 us
    all_to_all x1, starting transfers between devices, on_device(): lax.all_to_all(fo_copies, 'req', split_axis=0, concat_axis=0, tiled=True)  17.6 us
  transfers between devices with their start and end apart: 6, of which 6 were waited for; matrix products, arithmetic and copies ran while one was open for 5% of the time, Pallas kernels for 0%

profile of v1, /device:TPU:57, one launch (start us, length us, event | category | flops | bytes accessed | tf_op | source)
XLA Modules:
  0.0 804.6 jit_solution(10880859803325053617)
XLA Ops:
  6.5 1.0 convert_reduce_fusion.3
  7.5 0.7 multiply_add_fusion.1
  8.3 0.7 all_to_all.28
  9.0 10.6 %all-to-all-start = ((bf16[32,1,2]{2,1,0:T(2,128)(2,1)}), bf16[32,1,2]{2,1,0:T(2,128)(2,1)S(1)}, u32[]{:S(2)}, u32[]{:S(2)}) async-start(bf16[32,1,2]{2,1,0:T(2,128)(2,1)} %all_to_all.28), calls=%async_computation | async-start | bytes 32768 | tf_op jit(solution)/shard_map/all_to_all | solution.py:72
  19.7 1.0 copy.77
  20.7 0.4 convolution_convert_fusion.1
  21.1 1.1 reshape.357
  22.3 5.1 all-to-all-done
  27.4 4.7 all-to-all-start.1
  32.6 15.0 %all-to-all-done.1 = bf16[32,2,4096]{2,1,0:T(2,128)(2,1)S(1)} async-done(((bf16[32,2,4096]{2,1,0:T(2,128)(2,1)}), bf16[32,2,4096]{2,1,0:T(2,128)(2,1)S(1)}, u32[]{:S(2)}, u32[]{:S(2)}) %all-to-all-start.1) | async-done | bytes 524320 | tf_op jit(solution)/shard_map/all_to_all | solution.py:71
  47.6 0.2 reshape.358
  47.8 0.3 convolution_convert_fusion.3
  48.1 0.1 reshape.359
  48.2 0.1 copy.60
  48.4 1.5 broadcast_in_dim.15
  49.9 7.7 all-to-all-start.2
  57.8 24.4 %all-to-all-done.2 = bf16[8,256,512]{1,2,0:T(8,128)(2,1)} async-done(((bf16[8,256,512]{1,2,0:T(8,128)(2,1)}), bf16[8,256,512]{1,2,0:T(8,128)(2,1)}, u32[]{:S(2)}, u32[]{:S(2)}) %all-to-all-start.2) | async-done | bytes 2097184 | tf_op jit(solution)/shard_map/all_to_all | solution.py:87
  82.2 5.9 stack.20
  88.2 5.1 all-to-all-start.3
  93.3 0.1 copy.70
  93.4 386.5 %all-to-all-done.3 = bf16[32,128,2048]{2,1,0:T(8,128)(2,1)} async-done(((bf16[32,128,2048]{2,1,0:T(8,128)(2,1)}), bf16[32,128,2048]{2,1,0:T(8,128)(2,1)}, u32[]{:S(2)}, u32[]{:S(2)}) %all-to-all-start.3) | async-done | bytes 16777248 | tf_op jit(solution)/shard_map/all_to_all | solution.py:121
  479.9 4.3 broadcast_in_dim.19
  484.2 17.6 %all-to-all-start.4 = ((bf16[32,1024,128]{1,2,0:T(8,128)(2,1)}), bf16[32,1024,128]{1,2,0:T(8,128)(2,1)}, u32[]{:S(2)}, u32[]{:S(2)}) async-start(bf16[32,1024,128]{1,2,0:T(8,128)(2,1)} %broadcast_in_dim.19), calls=%async_computation.4 | async-start | bytes 16777216 | tf_op jit(solution)/shard_map/all_to_all | solution.py:119
  501.9 0.5 multiply_power_fusion
  502.5 0.2 select_reduce_fusion
  502.7 0.6 subtract_convert_fusion
  503.4 2.2 convert_reduce_fusion
  505.6 2.3 multiply_reduce_fusion
  507.9 2.6 fusion.5
  510.5 0.6 fusion.25
  511.1 0.6 fusion.29
  511.7 0.6 fusion.27
  512.2 0.4 multiply_reduce_fusion.2
  512.7 35.0 %all-reduce = (bf16[256,16]{0,1:T(8,128)(2,1)S(1)}, bf16[256,16]{0,1:T(8,128)(2,1)S(1)}, bf16[256,16]{0,1:T(8,128)(2,1)S(1)}) all-reduce(f32[256,16]{0,1:T(8,128)S(1)} %get-tuple-element.6, f32[256,16]{0,1:T(8,128)S(1)} %get-tuple-element.7, f32[256,16]{0,1:T(8,128)S(1)} %get-tuple-element.5), channel_id=1, replica_groups=mesh['req'=32,'mlp'=8] {'mlp'}, use_global_device_ids=true, to_apply=%region_14.15 | all-reduce | flops 12288 | bytes 73728 | tf_op jit(solution)/shard_map/psum | solution.py:103
  547.7 0.9 broadcast_multiply_fusion.1
  548.7 8.6 %fusion = f32[256,1792]{1,0:T(8,128)S(1)} fusion(bf16[256,4096]{0,1:T(8,128)(2,1)} %copy-done.1, bf16[4096,2048]{1,0:T(8,128)(2,1)} %bitcast.3), kind=kOutput, calls=%fused_computation | convolution fusion | flops 3758096384 | bytes 18612224 | tf_op jit(solution)/shard_map/dot_general | solution.py:124
  557.3 1.2 copy-done.2
  558.5 0.3 fusion.9
  558.8 1.2 slice.41
  560.1 1.9 slice.42
  562.0 1.0 slice_bitcast_fusion
  562.9 1.8 slice.45
  564.8 1.9 slice.46
  566.6 1.6 fusion.60
  568.3 0.7 pad_maximum_fusion
  569.0 1.6 copy.65
  570.6 1.4 concatenate.26
  572.0 1.5 copy.66
  573.5 0.7 copy.67
  574.2 0.8 concatenate.29
  575.1 0.1 fusion.47
  575.2 1.2 fusion.84
  576.5 1.6 fusion.10
  578.1 113.9 %all-to-all-done.4 = bf16[32,1024,128]{1,2,0:T(8,128)(2,1)} async-done(((bf16[32,1024,128]{1,2,0:T(8,128)(2,1)}), bf16[32,1024,128]{1,2,0:T(8,128)(2,1)}, u32[]{:S(2)}, u32[]{:S(2)}) %all-to-all-start.4) | async-done | bytes 8388640 | tf_op jit(solution)/shard_map/all_to_all | solution.py:119
  692.0 8.9 %fusion.17 = f32[256,4096]{1,0:T(8,128)} fusion(bf16[1024,4096]{0,1:T(8,128)(2,1)} %bitcast.22, bf16[256,1024]{0,1:T(8,128)(2,1)S(1)} %bitcast.78, bf16[1024,1024]{1,0:T(8,128)(2,1)S(1)} %copy-done, f32[256,1792]{1,0:T(8,128)} %copy-done.2, f32[1024]{0:T(1024)S(1)} %copy-done.15), kind=kOutput, calls=%fused_computation.34 | convolution fusion | flops 2687238144 | bytes 16257024 | tf_op jit(solution)/shard_map/reshape | solution.py:152
  700.9 5.8 convolution_add_fusion
  706.7 59.7 %reduce-scatter.2.cloned.1.call-done = f32[256,512]{1,0:T(8,128)} async-done(((f32[256,4096]{1,0:T(8,128)}), f32[256,512]{1,0:T(8,128)}) %reduce-scatter.2.cloned.1.call-update) | async-done | bytes 524304 | tf_op jit(solution)/shard_map/reduce_scatter | solution.py:153
  766.5 1.1 add_convert_fusion
  767.7 0.4 convolution_convert_fusion
  768.1 0.3 reshape.369
  768.5 26.9 %all_to_all.35 = bf16[32,2,4096]{2,1,0:T(2,128)(2,1)} all-to-all(bf16[32,2,4096]{2,1,0:T(2,128)(2,1)S(1)} %reshape.369), channel_id=1, replica_groups=mesh['req'=32,'mlp'=8] {'req'}, dimensions={0} | all-to-all | bytes 1048576 | tf_op jit(solution)/shard_map/all_to_all | solution.py:158
  795.4 1.2 reshape.370
  796.7 0.3 convolution_convert_fusion.2
  797.0 0.8 copy.78
  (69 shorter events, 1.4 us)
Async XLA Ops:
  6.5 685.5 %copy-start = (bf16[1024,1024]{1,0:T(8,128)(2,1)S(1)}, bf16[1024,1024]{1,0:T(8,128)(2,1)}, u32[]{:S(2)}) copy-start(bf16[1024,1024]{1,0:T(8,128)(2,1)} %param.37) | copy-start | bytes 6291460
  8.2 23.9 %copy-start.18 = (s32[32]{0:T(128)}, s32[32]{0:T(128)S(1)}, u32[]{:S(2)}) copy-start(s32[32]{0:T(128)S(1)} %multiply_add_fusion.1) | copy-start | bytes 388
  9.0 18.3 %all-to-all-start = ((bf16[32,1,2]{2,1,0:T(2,128)(2,1)}), bf16[32,1,2]{2,1,0:T(2,128)(2,1)S(1)}, u32[]{:S(2)}, u32[]{:S(2)}) async-start(bf16[32,1,2]{2,1,0:T(2,128)(2,1)} %all_to_all.28), calls=%async_computation | async-start | bytes 32768 | tf_op jit(solution)/shard_map/all_to_all | solution.py:72
  27.4 20.2 %all-to-all-start.1 = ((bf16[32,2,4096]{2,1,0:T(2,128)(2,1)}), bf16[32,2,4096]{2,1,0:T(2,128)(2,1)S(1)}, u32[]{:S(2)}, u32[]{:S(2)}) async-start(bf16[32,2,4096]{2,1,0:T(2,128)(2,1)} %reshape.357), calls=%async_computation.1 | async-start | bytes 1048576 | tf_op jit(solution)/shard_map/all_to_all | solution.py:71
  32.1 17.8 %copy-start.20 = (f32[32]{0:T(128)}, f32[32]{0:T(128)S(1)}, u32[]{:S(2)}) copy-start(f32[32]{0:T(128)S(1)} %iota_convert_fusion) | copy-start | bytes 388
  47.8 9.8 %copy-start.9 = (bf16[256,128]{1,0:T(8,128)(2,1)S(1)}, bf16[256,128]{1,0:T(8,128)(2,1)}, u32[]{:S(2)}) copy-start(bf16[256,128]{1,0:T(8,128)(2,1)} %param.29) | copy-start | bytes 196612
  47.8 9.9 %copy-start.10 = (bf16[128,256]{1,0:T(8,128)(2,1)S(1)}, bf16[128,256]{1,0:T(8,128)(2,1)}, u32[]{:S(2)}) copy-start(bf16[128,256]{1,0:T(8,128)(2,1)} %param.26) | copy-start | bytes 196612
  47.8 9.9 %copy-start.11 = (bf16[128,256]{1,0:T(8,128)(2,1)S(1)}, bf16[128,256]{1,0:T(8,128)(2,1)}, u32[]{:S(2)}) copy-start(bf16[128,256]{1,0:T(8,128)(2,1)} %param.27) | copy-start | bytes 196612
  48.1 9.7 %copy-start.12 = (bf16[128,256]{1,0:T(8,128)(2,1)S(1)}, bf16[128,256]{1,0:T(8,128)(2,1)}, u32[]{:S(2)}) copy-start(bf16[128,256]{1,0:T(8,128)(2,1)} %param.28) | copy-start | bytes 196612
  48.1 9.7 %copy-start.7 = (bf16[128,1024]{1,0:T(8,128)(2,1)S(1)}, bf16[128,1024]{1,0:T(8,128)(2,1)}, u32[]{:S(2)}) copy-start(bf16[128,1024]{1,0:T(8,128)(2,1)} %param.34) | copy-start | bytes 786436
  49.9 32.3 %all-to-all-start.2 = ((bf16[8,256,512]{1,2,0:T(8,128)(2,1)}), bf16[8,256,512]{1,2,0:T(8,128)(2,1)}, u32[]{:S(2)}, u32[]{:S(2)}) async-start(bf16[8,256,512]{1,2,0:T(8,128)(2,1)} %broadcast_in_dim.15), calls=%async_computation.2 | async-start | bytes 4194304 | tf_op jit(solution)/shard_map/all_to_all | solution.py:87
  88.2 5.1 copy-start.8
  88.2 391.7 %all-to-all-start.3 = ((bf16[32,128,2048]{2,1,0:T(8,128)(2,1)}), bf16[32,128,2048]{2,1,0:T(8,128)(2,1)}, u32[]{:S(2)}, u32[]{:S(2)}) async-start(bf16[32,128,2048]{2,1,0:T(8,128)(2,1)} %stack.20), calls=%async_computation.3 | async-start | bytes 33554432 | tf_op jit(solution)/shard_map/all_to_all | solution.py:121
  484.2 18.2 %copy-start.16 = (s32[256]{0:T(256)S(1)}, s32[256]{0:T(256)}, u32[]{:S(2)}) copy-start(s32[256]{0:T(256)} %param.22) | copy-start | bytes 3076
  484.2 18.4 %copy-start.22 = (s32[256]{0:T(256)S(1)}, s32[256]{0:T(256)}, u32[]{:S(2)}) copy-start(s32[256]{0:T(256)} %param.23) | copy-start | bytes 3076
  484.2 207.8 %all-to-all-start.4 = ((bf16[32,1024,128]{1,2,0:T(8,128)(2,1)}), bf16[32,1024,128]{1,2,0:T(8,128)(2,1)}, u32[]{:S(2)}, u32[]{:S(2)}) async-start(bf16[32,1024,128]{1,2,0:T(8,128)(2,1)} %broadcast_in_dim.19), calls=%async_computation.4 | async-start | bytes 16777216 | tf_op jit(solution)/shard_map/all_to_all | solution.py:119
  501.8 6.1 copy-start.13
  501.8 6.1 copy-start.14
  501.8 264.6 %reduce-scatter.2.cloned.1.call-start = ((), (), s32[]{:S(2)}) async-start(), calls=%async_computation.7 | async-start | bytes 4718592 | tf_op jit(solution)/shard_map/reduce_scatter | solution.py:153
  503.3 7.2 copy-start.3
  505.6 5.5 copy-start.4
  507.9 3.8 copy-start.5
  510.5 2.2 copy-start.1
  548.7 9.8 %copy-start.6 = (bf16[1024,256]{1,0:T(8,128)(2,1)S(1)}, bf16[1024,256]{1,0:T(8,128)(2,1)}, u32[]{:S(2)}) copy-start(bf16[1024,256]{1,0:T(8,128)(2,1)} %param.31) | copy-start | bytes 1572868
  557.3 1.2 copy-start.2
  557.3 134.7 %copy-start.15 = (f32[1024]{0:T(1024)S(1)}, f32[1024]{0:T(1024)}, u32[]{:S(2)}) copy-start(f32[1024]{0:T(1024)} %param.35) | copy-start | bytes 12292
  706.7 59.8 %copy-start.17 = (f32[512]{0:T(512)S(1)}, f32[512]{0:T(512)}, u32[]{:S(2)}) copy-start(f32[512]{0:T(512)} %param.39) | copy-start | bytes 6148
  706.7 61.0 %copy-start.21 = (f32[32]{0:T(128)S(1)}, f32[32]{0:T(128)}, u32[]{:S(2)}) copy-start(f32[32]{0:T(128)} %copy-done.20) | copy-start | bytes 388
  706.7 90.0 %copy-start.19 = (s32[32]{0:T(128)S(1)}, s32[32]{0:T(128)}, u32[]{:S(2)}) copy-start(s32[32]{0:T(128)} %copy-done.18) | copy-start | bytes 388
Sparse Core Ops, SparseCore 0:
  706.8 59.5 reduce-scatter.1
